TPU v7x, 256 devices: a whole 4x4x8 slice. The times are simulated.
256 devices in a mesh: group: 2 (over core), dp: 16 (over y, x), tensor: 8 (over z).
Axes of the slice: x: 4, y: 4, z: 8, core: 2. Of those that a mesh axis runs over, the one named last changes fastest.
Arguments:
- stream: bfloat16 [512, 8192], P('tensor', ('group', 'dp'))
- norm_attn: bfloat16 [8192], P(('group', 'dp')), may hold values from 0.29882812 to 3
- norm_ffn: bfloat16 [8192], P(('group', 'dp')), may hold values from 0.29882812 to 3
- w_query: bfloat16 [8192, 8192], P(('group', 'dp'), 'tensor'), may hold values from -0.0625 to 0.0625
- w_keyval: bfloat16 [8192, 2048], P(('group', 'dp'), 'tensor'), may hold values from -0.0625 to 0.0625
- w_out: bfloat16 [8192, 8192], P('tensor', ('group', 'dp')), may hold values from -0.0625 to 0.0625
- w_gate: bfloat16 [8192, 28672], P(('group', 'dp'), 'tensor'), may hold values from -0.0625 to 0.0625
- w_up: bfloat16 [8192, 28672], P(('group', 'dp'), 'tensor'), may hold values from -0.0625 to 0.0625
- w_down: bfloat16 [28672, 8192], P('tensor', ('group', 'dp')), may hold values from -0.03125 to 0.03125
- cache: bfloat16 [512, 8, 256, 256], P(('group', 'dp'), 'tensor')
- lengths: int32 [512], P(('group', 'dp')), may hold values from 1 to 256, as said below
- location: int32 [512], P(('group', 'dp')), may hold values from 0 to 511, as said below
Outputs:
- updated: float32 [512, 8192], P('tensor', ('group', 'dp'))
Inputs may be any that keep to these rules, and one draw needn't show every extreme that they name: Each of the 512 slots is named by exactly one request. Slot s belongs to owner s // 16. Requests r of one aligned block of 16 (one device's requests) that share an owner have different values of location modulo 2; in every draw 2 of them share an owner. `lengths`: some slot holds 256 valid positions in every draw.
All inputs are finite; a program needn't handle non-finite values.
Results may differ from a plain program's by a relative error of at most 0.005.
The roundings to bfloat16 on the way count: a program that leaves them out, or rounds other values in their place, can miss the bound.
Values may be sent and summed in bfloat16 or wider, within the bound.
No kernel may reach another device: no remote copies, remote signals or barrier semaphores. Data moves between devices by JAX's collectives and lax.ppermute only.
A program may use at most 64 MiB of HBM per device.

v0:
```python
import jax
import jax.numpy as jnp
from jax import lax
from jax.sharding import PartitionSpec as P

D = 8192
WIDTH = ("group", "dp")
EPSILON = 1e-05


def gather_width(values):
    owners = lax.axis_size(WIDTH)
    sent = jnp.broadcast_to(values[None], (owners,) + values.shape)
    return lax.all_to_all(sent, WIDTH, 0, 0, tiled=True)


def scale_rows(values, squares, gain):
    scale = lax.rsqrt(squares / D + EPSILON)
    return (values * scale[:, None] * gain.astype(jnp.float32)[None, :]).astype(jnp.bfloat16)


def gather_rows(values):
    chips = lax.axis_size("dp")
    across = lax.all_to_all(
        jnp.broadcast_to(values[None], (chips,) + values.shape), "dp", 0, 0, tiled=True
    )
    cores = lax.axis_size("group")
    both = lax.all_to_all(
        jnp.broadcast_to(across[None], (cores,) + across.shape), "group", 0, 0, tiled=True
    )
    return both.reshape((-1,) + values.shape[1:])


def reduce_chips(partial, link_type):
    chips = lax.axis_size("dp")
    blocks = partial.reshape((chips, partial.shape[0] // chips) + partial.shape[1:])
    moved = lax.all_to_all(blocks.astype(link_type), "dp", 0, 0, tiled=True)
    return jnp.sum(moved.astype(jnp.float32), axis=0)


def chip_blocks(values):
    cores = lax.axis_size("group")
    parts = lax.axis_size("tensor")
    sent = jnp.broadcast_to(values[None], (cores * parts,) + values.shape)
    got = lax.all_to_all(sent, ("group", "tensor"), 0, 0, tiled=True)
    return got.reshape((cores, parts) + values.shape)


def chip_rows(values):
    blocks = chip_blocks(values)
    cores, parts, rows, width = blocks.shape
    return blocks.transpose(1, 2, 0, 3).reshape(parts * rows, cores * width)


def chip_weights(matrices):
    return lax.all_gather(jnp.concatenate(matrices, axis=1), "group", axis=0, tiled=True)


def reduce_rows(partial, axis):
    parts = lax.axis_size(axis)
    blocks = partial.reshape((parts, partial.shape[0] // parts) + partial.shape[1:])
    return jnp.sum(lax.all_to_all(blocks, axis, 0, 0, tiled=True), axis=0)


def attend(query, fresh, stored, counts):
    items = query.shape[0]
    kv_local = stored.shape[1]
    head_size = stored.shape[3] // 2
    grouped = query.reshape(items, kv_local, -1, head_size)
    fresh = fresh.reshape(items, kv_local, 2 * head_size)
    scale = head_size ** (-0.5)
    scores = (
        jnp.einsum(
            "mkgd,mkpd->mkgp", grouped, stored[..., :head_size], preferred_element_type=jnp.float32
        )
        * scale
    )
    own = (
        jnp.einsum(
            "mkgd,mkd->mkg", grouped, fresh[..., :head_size], preferred_element_type=jnp.float32
        )
        * scale
    )
    place = jnp.arange(stored.shape[2], dtype=jnp.int32)
    valid = place[None, None, None, :] < counts[:, None, None, None]
    top = jnp.maximum(jnp.max(jnp.where(valid, scores, -1e30), axis=3), own)
    expo = jnp.where(valid, jnp.exp(scores - top[..., None]), 0.0)
    own_expo = jnp.exp(own - top)
    total = jnp.sum(expo, axis=3) + own_expo
    probs = (expo / total[..., None]).astype(jnp.bfloat16)
    own_prob = (own_expo / total).astype(jnp.bfloat16)
    mixed = jnp.einsum(
        "mkgp,mkpd->mkgd", probs, stored[..., head_size:], preferred_element_type=jnp.float32
    )
    mixed = mixed + own_prob.astype(jnp.float32)[..., None] * fresh[:, :, None, head_size:].astype(
        jnp.float32
    )
    return mixed.reshape(items, -1).astype(jnp.bfloat16)


def per_device(
    stream,
    norm_attn,
    norm_ffn,
    w_query,
    w_keyval,
    w_out,
    w_gate,
    w_up,
    w_down,
    cache,
    lengths,
    location,
):
    rows = stream.shape[0]
    resid = stream.astype(jnp.float32)
    width = stream.shape[1]
    parts = lax.axis_size("tensor")
    per_owner = location.shape[0]
    pieces = jnp.concatenate([location // per_owner, location % per_owner]).astype(jnp.bfloat16)
    extra = jnp.zeros((width,), jnp.bfloat16).at[: 2 * per_owner].set(pieces)
    blocks = chip_blocks(jnp.concatenate([stream, norm_attn[None, :], extra[None, :]], axis=0))
    cores = blocks.shape[0]
    raw = blocks[:, :, :rows].transpose(1, 2, 0, 3).reshape(parts * rows, cores * width)
    raw = raw.astype(jnp.float32)
    gain = blocks[:, 0, rows].reshape(-1)
    halves = (
        blocks[:, 0, rows + 1, : 2 * per_owner].astype(jnp.float32).reshape(cores, 2, per_owner)
    )
    chip_where = halves[:, 0] * per_owner + halves[:, 1]
    chip_squares = jnp.sum(raw * raw, axis=1)
    chips = lax.axis_size("dp")
    payload = jnp.concatenate([chip_squares, chip_where.reshape(-1)])
    shared = lax.all_to_all(
        jnp.broadcast_to(payload[None], (chips, payload.shape[0])), "dp", 0, 0, tiled=True
    )
    requests = chip_squares.shape[0]
    all_squares = jnp.sum(shared[:, :requests], axis=0)
    where = shared[:, requests:].reshape(chips, cores, per_owner).transpose(1, 0, 2)
    where = where.reshape(-1).astype(jnp.int32)
    by_slot = jnp.zeros((requests,), jnp.int32).at[where].set(jnp.arange(requests, dtype=jnp.int32))
    core = lax.axis_index("group")
    half = requests // lax.axis_size("group")
    qkv_weights = chip_weights((w_query, w_keyval))
    ffn_weights = chip_weights((w_gate, w_up))
    mine = lax.dynamic_slice_in_dim(by_slot, core * half, half)
    gathered = scale_rows(raw[mine], all_squares[mine], gain)
    joined = jnp.dot(gathered, qkv_weights, preferred_element_type=jnp.float32)
    summed = reduce_chips(joined, jnp.float32)
    query_cols = w_query.shape[1]
    query = summed[:, :query_cols].astype(jnp.bfloat16)
    fresh = summed[:, query_cols:].astype(jnp.bfloat16)
    answer = attend(query, fresh, cache, lengths)
    attended = gather_rows(answer)
    mixed = jnp.dot(attended, w_out, preferred_element_type=jnp.float32)[where]
    middle = resid + reduce_rows(mixed, "tensor")
    squares = jnp.sum(gather_width(jnp.sum(middle * middle, axis=1)), axis=0)
    ffn_in = scale_rows(middle, squares, norm_ffn)
    gathered = lax.dynamic_slice_in_dim(chip_rows(ffn_in), core * half, half)
    both = reduce_chips(
        jnp.dot(gathered, ffn_weights, preferred_element_type=jnp.float32), jnp.bfloat16
    )
    hidden_cols = w_gate.shape[1]
    hidden = (jax.nn.silu(both[:, :hidden_cols]) * both[:, hidden_cols:]).astype(jnp.bfloat16)
    hidden = gather_rows(hidden)
    down = jnp.dot(hidden, w_down, preferred_element_type=jnp.float32)
    return middle + reduce_rows(down, "tensor")


def solution(mesh):
    placed = (
        P("tensor", WIDTH),
        P(WIDTH),
        P(WIDTH),
        P(WIDTH, "tensor"),
        P(WIDTH, "tensor"),
        P("tensor", WIDTH),
        P(WIDTH, "tensor"),
        P(WIDTH, "tensor"),
        P("tensor", WIDTH),
        P(WIDTH, "tensor", None, None),
        P(WIDTH),
        P(WIDTH),
    )
    return jax.shard_map(
        per_device, mesh=mesh, in_specs=placed, out_specs=P("tensor", WIDTH), check_vma=False
    )
```

profile of v0, /device:TPU:1, one launch (start us, length us, event | category | flops | bytes accessed | tf_op | source)
XLA Modules:
  0.0 287.4 jit_solution(8751193857991613794)
XLA Ops:
  6.5 2.1 pad_maximum_fusion.1
  11.8 10.0 %all-to-all-start = ((bf16[16,66,256]{2,1,0:T(8,128)(2,1)}), bf16[16,66,256]{2,1,0:T(8,128)(2,1)S(1)}, u32[]{:S(2)}, u32[]{:S(2)}) async-start(bf16[16,66,256]{2,1,0:T(8,128)(2,1)} %broadcast_in_dim.40), calls=%async_computation | async-start | bytes 1179648 | tf_op jit(solution)/shard_map/all_to_all | solution.py:45
  21.8 4.3 %pad_maximum_fusion = bf16[256,7168]{1,0:T(8,128)(2,1)} fusion(bf16[256,3584]{1,0:T(8,128)(2,1)} %param.21, bf16[256,3584]{1,0:T(8,128)(2,1)} %param.20), kind=kLoop, calls=%fused_computation.6 | loop fusion | flops 7340032 | bytes 7340032 | tf_op jit(solution)/shard_map/concatenate | solution.py:56
  26.2 11.5 %all-to-all-done = bf16[16,66,256]{2,1,0:T(8,128)(2,1)S(1)} async-done(((bf16[16,66,256]{2,1,0:T(8,128)(2,1)}), bf16[16,66,256]{2,1,0:T(8,128)(2,1)S(1)}, u32[]{:S(2)}, u32[]{:S(2)}) %all-to-all-start) | async-done | bytes 540704 | tf_op jit(solution)/shard_map/all_to_all | solution.py:45
  39.1 6.8 %all-to-all-start.1 = ((f32[16,1,544]{2,1,0:T(1,128)}), f32[16,1,544]{2,1,0:T(1,128)S(1)}, u32[]{:S(2)}, u32[]{:S(2)}) async-start(f32[16,1,544]{2,1,0:T(1,128)} %broadcast_in_dim.41), calls=%async_computation.1 | async-start | bytes 81920 | tf_op jit(solution)/shard_map/all_to_all | solution.py:134
  46.5 5.8 %all-to-all-done.1 = f32[16,1,544]{2,1,0:T(1,128)S(1)} async-done(((f32[16,1,544]{2,1,0:T(1,128)}), f32[16,1,544]{2,1,0:T(1,128)S(1)}, u32[]{:S(2)}, u32[]{:S(2)}) %all-to-all-start.1) | async-done | bytes 34848 | tf_op jit(solution)/shard_map/all_to_all | solution.py:134
  52.5 2.4 scatter_custom_fusion
  56.1 1.9 gather_fusion.1
  58.1 3.0 %fusion.4 = f32[256,1280]{1,0:T(8,128)} fusion(bf16[512,1280]{1,0:T(8,128)(2,1)} %all-gather.3.cloned.1.call-done, f32[256,512]{1,0:T(8,128)S(1)} %gather_fusion, f32[512]{0:T(512)S(1)} %bitcast.94, f32[256]{0:T(256)S(1)} %add_rsqrt_fusion), kind=kOutput, calls=%fused_computation.20 | convolution fusion | flops 335937536 | bytes 3148800 | tf_op jit(solution)/shard_map/dot_general | solution.py:148
  61.1 3.8 %all-to-all-start.2 = ((f32[16,16,1280]{2,1,0:T(8,128)}), f32[16,16,1280]{2,1,0:T(8,128)S(1)}, u32[]{:S(2)}, u32[]{:S(2)}) async-start(f32[16,16,1280]{2,1,0:T(8,128)} %bitcast.7), calls=%async_computation.2 | async-start | bytes 2621440 | tf_op jit(solution)/shard_map/all_to_all | solution.py:37
  65.0 17.3 %all-to-all-done.2 = f32[16,16,1280]{2,1,0:T(8,128)S(1)} async-done(((f32[16,16,1280]{2,1,0:T(8,128)}), f32[16,16,1280]{2,1,0:T(8,128)S(1)}, u32[]{:S(2)}, u32[]{:S(2)}) %all-to-all-start.2) | async-done | bytes 1310752 | tf_op jit(solution)/shard_map/all_to_all | solution.py:37
  82.6 1.7 select_reduce_fusion
  86.9 5.4 %all-to-all-start.3 = ((bf16[16,16,1024]{2,1,0:T(8,128)(2,1)}), bf16[16,16,1024]{2,1,0:T(8,128)(2,1)S(1)}, u32[]{:S(2)}, u32[]{:S(2)}) async-start(bf16[16,16,1024]{2,1,0:T(8,128)(2,1)} %broadcast_in_dim.45), calls=%async_computation.3 | async-start | bytes 1048576 | tf_op jit(solution)/shard_map/all_to_all | solution.py:24
  92.4 9.5 %all-to-all-done.3 = bf16[16,16,1024]{2,1,0:T(8,128)(2,1)S(1)} async-done(((bf16[16,16,1024]{2,1,0:T(8,128)(2,1)}), bf16[16,16,1024]{2,1,0:T(8,128)(2,1)S(1)}, u32[]{:S(2)}, u32[]{:S(2)}) %all-to-all-start.3) | async-done | bytes 524320 | tf_op jit(solution)/shard_map/all_to_all | solution.py:24
  102.0 7.2 %all_to_all.65 = bf16[2,16,16,1024]{3,2,1,0:T(8,128)(2,1)S(1)} all-to-all(bf16[2,16,16,1024]{3,2,1,0:T(8,128)(2,1)S(1)} %broadcast_in_dim.46), channel_id=1, replica_groups=mesh['group'=2,'dp'=16,'tensor'=8] {'group'}, dimensions={0} | all-to-all | bytes 2097152 | tf_op jit(solution)/shard_map/all_to_all | solution.py:28
  111.3 22.7 %all_to_all.66 = f32[8,64,256]{2,1,0:T(8,128)S(1)} all-to-all(f32[8,64,256]{2,1,0:T(8,128)S(1)} %bitcast.78), channel_id=1, replica_groups=mesh['group'=2,'dp'=16,'tensor'=8] {'tensor'}, dimensions={0} | all-to-all | bytes 1048576 | tf_op jit(solution)/shard_map/all_to_all | solution.py:62
  134.7 5.3 %all-to-all-start.6 = ((f32[32,1,64]{2,1,0:T(1,128)}), f32[32,1,64]{2,1,0:T(1,128)S(1)}, u32[]{:S(2)}, u32[]{:S(2)}) async-start(f32[32,1,64]{2,1,0:T(1,128)} %broadcast_in_dim.47), calls=%async_computation.6 | async-start | bytes 32768 | tf_op jit(solution)/shard_map/all_to_all | solution.py:14
  140.1 6.7 %all-to-all-done.6 = f32[32,1,64]{2,1,0:T(1,128)S(1)} async-done(((f32[32,1,64]{2,1,0:T(1,128)}), f32[32,1,64]{2,1,0:T(1,128)S(1)}, u32[]{:S(2)}, u32[]{:S(2)}) %all-to-all-start.6) | async-done | bytes 8224 | tf_op jit(solution)/shard_map/all_to_all | solution.py:14
  147.0 18.0 %all_to_all.67 = bf16[16,64,256]{2,1,0:T(8,128)(2,1)S(1)} all-to-all(bf16[16,64,256]{2,1,0:T(8,128)(2,1)S(1)} %broadcast_in_dim.48), channel_id=1, replica_groups=mesh['group'=2,'dp'=16,'tensor'=8] {'group','tensor'}, dimensions={0} | all-to-all | bytes 1048576 | tf_op jit(solution)/shard_map/all_to_all | solution.py:45
  165.6 5.2 %convolution_convert_fusion = bf16[256,7168]{1,0:T(8,128)(2,1)S(1)} fusion(bf16[512,7168]{1,0:T(8,128)(2,1)} %all-gather.5.cloned.1.call-done, bf16[512,512]{1,0:T(8,128)(2,1)S(1)} %bitcast.83, s32[]{:T(128)S(6)} %select_n.43), kind=kOutput, calls=%fused_computation.4 | convolution fusion | flops 1880883200 | bytes 11272196 | tf_op jit(solution)/shard_map/dot_general | solution.py:161
  170.8 46.8 %all_to_all.68 = bf16[16,16,7168]{2,1,0:T(8,128)(2,1)S(1)} all-to-all(bf16[16,16,7168]{2,1,0:T(8,128)(2,1)S(1)} %bitcast.76), channel_id=1, replica_groups=mesh['group'=2,'dp'=16,'tensor'=8] {'dp'}, dimensions={0} | all-to-all | bytes 7340032 | tf_op jit(solution)/shard_map/all_to_all | solution.py:37
  218.4 26.6 %all_to_all.69 = bf16[16,16,3584]{2,1,0:T(8,128)(2,1)S(1)} all-to-all(bf16[16,16,3584]{2,1,0:T(8,128)(2,1)S(1)} %broadcast_in_dim.49), channel_id=1, replica_groups=mesh['group'=2,'dp'=16,'tensor'=8] {'dp'}, dimensions={0} | all-to-all | bytes 3670016 | tf_op jit(solution)/shard_map/all_to_all | solution.py:24
  245.4 9.5 %all_to_all.70 = bf16[2,16,16,3584]{3,2,1,0:T(8,128)(2,1)S(1)} all-to-all(bf16[2,16,16,3584]{3,2,1,0:T(8,128)(2,1)S(1)} %broadcast_in_dim.50), channel_id=1, replica_groups=mesh['group'=2,'dp'=16,'tensor'=8] {'group'}, dimensions={0} | all-to-all | bytes 7340032 | tf_op jit(solution)/shard_map/all_to_all | solution.py:28
  256.0 23.8 %all_to_all.71 = f32[8,64,256]{2,1,0:T(8,128)S(1)} all-to-all(f32[8,64,256]{2,1,0:T(8,128)S(1)} %fusion), channel_id=1, replica_groups=mesh['group'=2,'dp'=16,'tensor'=8] {'tensor'}, dimensions={0} | all-to-all | bytes 1048576 | tf_op jit(solution)/shard_map/all_to_all | solution.py:62
  (81 shorter events, 16.1 us)
Async XLA Ops:
  6.5 248.4 %copy-start = (bf16[3584,256]{1,0:T(8,128)(2,1)S(1)}, bf16[3584,256]{1,0:T(8,128)(2,1)}, u32[]{:S(2)}) copy-start(bf16[3584,256]{1,0:T(8,128)(2,1)} %param.22) | copy-start | bytes 5505028
  6.5 51.5 %all-gather.3.cloned.1.call-start = ((), (), s32[]{:S(2)}) async-start(), calls=%async_computation.12 | async-start | bytes 1966080 | tf_op jit(solution)/shard_map/all_gather | solution.py:56
  11.8 25.9 %all-to-all-start = ((bf16[16,66,256]{2,1,0:T(8,128)(2,1)}), bf16[16,66,256]{2,1,0:T(8,128)(2,1)S(1)}, u32[]{:S(2)}, u32[]{:S(2)}) async-start(bf16[16,66,256]{2,1,0:T(8,128)(2,1)} %broadcast_in_dim.40), calls=%async_computation | async-start | bytes 1179648 | tf_op jit(solution)/shard_map/all_to_all | solution.py:45
  21.8 143.9 %all-gather.5.cloned.1.call-start = ((), (), s32[]{:S(2)}) async-start(), calls=%async_computation.13 | async-start | bytes 11010048 | tf_op jit(solution)/shard_map/all_gather | solution.py:56
  39.1 13.2 %all-to-all-start.1 = ((f32[16,1,544]{2,1,0:T(1,128)}), f32[16,1,544]{2,1,0:T(1,128)S(1)}, u32[]{:S(2)}, u32[]{:S(2)}) async-start(f32[16,1,544]{2,1,0:T(1,128)} %broadcast_in_dim.41), calls=%async_computation.1 | async-start | bytes 81920 | tf_op jit(solution)/shard_map/all_to_all | solution.py:134
  61.1 3.8 %copy-start.3 = (s32[16]{0:T(128)S(1)}, s32[16]{0:T(128)}, u32[]{:S(2)}) copy-start(s32[16]{0:T(128)} %param.24) | copy-start | bytes 196
  61.1 21.2 %all-to-all-start.2 = ((f32[16,16,1280]{2,1,0:T(8,128)}), f32[16,16,1280]{2,1,0:T(8,128)S(1)}, u32[]{:S(2)}, u32[]{:S(2)}) async-start(f32[16,16,1280]{2,1,0:T(8,128)} %bitcast.7), calls=%async_computation.2 | async-start | bytes 2621440 | tf_op jit(solution)/shard_map/all_to_all | solution.py:37
  86.9 15.0 %all-to-all-start.3 = ((bf16[16,16,1024]{2,1,0:T(8,128)(2,1)}), bf16[16,16,1024]{2,1,0:T(8,128)(2,1)S(1)}, u32[]{:S(2)}, u32[]{:S(2)}) async-start(bf16[16,16,1024]{2,1,0:T(8,128)(2,1)} %broadcast_in_dim.45), calls=%async_computation.3 | async-start | bytes 1048576 | tf_op jit(solution)/shard_map/all_to_all | solution.py:24
  92.3 16.9 %copy-start.2 = (bf16[1024,256]{1,0:T(8,128)(2,1)S(1)}, bf16[1024,256]{1,0:T(8,128)(2,1)}, u32[]{:S(2)}) copy-start(bf16[1024,256]{1,0:T(8,128)(2,1)} %param.19) | copy-start | bytes 1572868
  109.7 24.3 %copy-start.1 = (bf16[64,256]{1,0:T(8,128)(2,1)S(1)}, bf16[64,256]{1,0:T(8,128)(2,1)}, u32[]{:S(2)}) copy-start(bf16[64,256]{1,0:T(8,128)(2,1)} %param.14) | copy-start | bytes 98308
  109.7 30.4 %copy-start.4 = (bf16[256]{0:T(256)(128)(2,1)S(1)}, bf16[256]{0:T(256)(128)(2,1)}, u32[]{:S(2)}) copy-start(bf16[256]{0:T(256)(128)(2,1)} %param.16) | copy-start | bytes 1540
  134.7 12.1 %all-to-all-start.6 = ((f32[32,1,64]{2,1,0:T(1,128)}), f32[32,1,64]{2,1,0:T(1,128)S(1)}, u32[]{:S(2)}, u32[]{:S(2)}) async-start(f32[32,1,64]{2,1,0:T(1,128)} %broadcast_in_dim.47), calls=%async_computation.6 | async-start | bytes 32768 | tf_op jit(solution)/shard_map/all_to_all | solution.py:14
Sparse Core Ops, SparseCore 0:
  9.1 19.2 all-gather.2
  30.2 24.9 all-gather.4
where the time goes:
time: 288 us; the launch traced here: 287 us
  blocking collectives  155 us (54%)
  waiting for transfers between devices  51 us (18%)
  starting transfers between devices  31.3 us (11%)
  between operations  13.8 us (5%)
  local copies, waits for them, and re-layouts  13.3 us (5%)
  matrix products  13.1 us (5%)
  other arithmetic  10.4 us (4%)
    all_to_all x1, blocking collectives, reduce_chips(): moved = lax.all_to_all(blocks.astype(link_type), 'dp', 0, 0, tiled=True)  46.8 us
    all_to_all x2, blocking collectives, reduce_rows(): return jnp.sum(lax.all_to_all(blocks, axis, 0, 0, tiled=True), axis=0)  46.5 us
    all_to_all x1, blocking collectives, gather_rows(): lax.all_to_all(jnp.broadcast_to(values[None], (chips,) + values.shape), '...  26.6 us
    all_to_all x1, blocking collectives, chip_blocks(): got = lax.all_to_all(sent, ('group', 'tensor'), 0, 0, tiled=True)  18 us
    all_to_all x1, waiting for transfers between devices, reduce_chips(): moved = lax.all_to_all(blocks.astype(link_type), 'dp', 0, 0, tiled=True)  17.3 us
    all_to_all x2, blocking collectives, gather_rows(): lax.all_to_all(jnp.broadcast_to(across[None], (cores,) + across.shape), '...  16.7 us
    all_to_all x1, waiting for transfers between devices, chip_blocks(): got = lax.all_to_all(sent, ('group', 'tensor'), 0, 0, tiled=True)  11.5 us
    all_to_all x1, starting transfers between devices, chip_blocks(): got = lax.all_to_all(sent, ('group', 'tensor'), 0, 0, tiled=True)  9.97 us
  transfers between devices with their start and end apart: 7, of which 5 were waited for; matrix products, arithmetic and copies ran while one was open for 9% of the time, Pallas kernels for 0%

commit v1 on v0

--- a/solution.py
+++ b/solution.py
@@ -6,6 +6,38 @@
 D = 8192
 WIDTH = ("group", "dp")
 EPSILON = 1e-05
+
+
+def step_on_the_page(view, k_dim, x_part):
+    frame_out = view.shape
+    new = view.reshape(
+        *frame_out[:k_dim], x_part, frame_out[k_dim] // x_part, *frame_out[k_dim + 1 :]
+    )
+    return jnp.moveaxis(new, k_dim, 0)
+
+
+def shelves_lead(page, array_dim):
+    m_next = list(page.shape[1:])
+    m_next[array_dim] *= page.shape[0]
+    return jnp.moveaxis(page, 0, array_dim).reshape(m_next)
+
+
+def derive_the_heaps(incoming_x, peer_axis, block_in, own_rows):
+    built = lax.psum(1, peer_axis)
+    val2 = lax.axis_index(peer_axis)
+    e_next, upper = (built, val2)
+    parts_out = step_on_the_page(incoming_x, block_in, e_next)
+    windows = [parts_out[upper]]
+    for num in range(1, e_next):
+        all_values = parts_out[upper ^ num]
+        windows.append(
+            lax.ppermute(
+                all_values, axis_name=peer_axis, perm=[(w, w ^ num) for w in range(e_next)]
+            )
+        )
+    state_now = jnp.stack(windows, axis=0)
+    parts_out = state_now[upper ^ jnp.arange(e_next)]
+    return shelves_lead(parts_out, own_rows)
 
 
 def gather_width(values):
@@ -42,7 +74,7 @@
     cores = lax.axis_size("group")
     parts = lax.axis_size("tensor")
     sent = jnp.broadcast_to(values[None], (cores * parts,) + values.shape)
-    got = lax.all_to_all(sent, ("group", "tensor"), 0, 0, tiled=True)
+    got = derive_the_heaps(sent, ("group", "tensor"), 0, 0)
     return got.reshape((cores, parts) + values.shape)
 
 

time: 288 us -> 374 us (1.30)
  starting transfers between devices: 31.3 us -> 87.3 us
  waiting for transfers between devices: 51 us -> 95 us
  blocking collectives: 155 us -> 135 us
    ppermute x0 -> x30, starting transfers between devices: none -> 66.9 us  [derive_the_heaps(): lax.ppermute(all_values, axis_name=peer_axis, perm=[(w, w ^ num) for w in...]
    ppermute x0 -> x30, waiting for transfers between devices: none -> 60.8 us  [derive_the_heaps(): lax.ppermute(all_values, axis_name=peer_axis, perm=[(w, w ^ num) for w in...]
    all_to_all x1 -> x0, blocking collectives: 18 us -> none  [chip_blocks(): got = lax.all_to_all(sent, ('group', 'tensor'), 0, 0, tiled=True)]
    all_to_all x1 -> x0, waiting for transfers between devices: 11.5 us -> none  [chip_blocks(): got = lax.all_to_all(sent, ('group', 'tensor'), 0, 0, tiled=True)]
    all_to_all x1 -> x0, starting transfers between devices: 9.97 us -> none  [chip_blocks(): got = lax.all_to_all(sent, ('group', 'tensor'), 0, 0, tiled=True)]
    all_to_all x1, waiting for transfers between devices: 17.3 us -> 13 us  [reduce_chips(): moved = lax.all_to_all(blocks.astype(link_type), 'dp', 0, 0, tiled=True)]
  transfers between devices with their start and end apart: 7 -> 36, of which waited for: 5 -> 25; matrix products, arithmetic and copies ran while one was open for 9% -> 7% of each run, Pallas kernels for 0% -> 0%
where the time goes in v1:
time: 374 us; the launch traced here: 373 us
  blocking collectives  135 us (36%)
  waiting for transfers between devices  95 us (25%)
  starting transfers between devices  87.3 us (23%)
  local copies, waits for them, and re-layouts  14.9 us (4%)
  between operations  13.9 us (4%)
  other arithmetic  13.5 us (4%)
  matrix products  13.3 us (4%)
    ppermute x30, starting transfers between devices, derive_the_heaps(): lax.ppermute(all_values, axis_name=peer_axis, perm=[(w, w ^ num) for w in...  66.9 us
    ppermute x30, waiting for transfers between devices, derive_the_heaps(): lax.ppermute(all_values, axis_name=peer_axis, perm=[(w, w ^ num) for w in...  60.8 us
    all_to_all x1, blocking collectives, reduce_chips(): moved = lax.all_to_all(blocks.astype(link_type), 'dp', 0, 0, tiled=True)  47.3 us
    all_to_all x2, blocking collectives, reduce_rows(): return jnp.sum(lax.all_to_all(blocks, axis, 0, 0, tiled=True), axis=0)  44 us
    all_to_all x1, blocking collectives, gather_rows(): lax.all_to_all(jnp.broadcast_to(values[None], (chips,) + values.shape), '...  27.2 us
    all_to_all x2, blocking collectives, gather_rows(): lax.all_to_all(jnp.broadcast_to(across[None], (cores,) + across.shape), '...  16.2 us
    all_to_all x1, waiting for transfers between devices, reduce_chips(): moved = lax.all_to_all(blocks.astype(link_type), 'dp', 0, 0, tiled=True)  13 us
    all_to_all x1, waiting for transfers between devices, gather_rows(): lax.all_to_all(jnp.broadcast_to(values[None], (chips,) + values.shape), '...  9.29 us
  transfers between devices with their start and end apart: 36, of which 25 were waited for; matrix products, arithmetic and copies ran while one was open for 7% of the time, Pallas kernels for 0%

profile of v1, /device:TPU:1, one launch (start us, length us, event | category | flops | bytes accessed | tf_op | source)
XLA Modules:
  0.0 372.7 jit_solution(13926027872821718137)
XLA Ops:
  8.8 7.0 %collective-permute-start.14 = (bf16[1,66,256]{2,1,0:T(8,128)(2,1)S(1)}, bf16[1,66,256]{2,1,0:T(8,128)(2,1)S(1)}, u32[]{:S(2)}, u32[]{:S(2)}) collective-permute-start(bf16[1,66,256]{2,1,0:T(8,128)(2,1)S(1)} %fusion.14), channel_id=1, source_target_pairs={{0,135},{1,134},{2,133},{3,132},{4,131},{5,130},{6,129},{7,128},{1... | collective-permute-start | bytes 101384 | tf_op jit(solution)/shard_map/ppermute | solution.py:34
  42.4 5.5 %collective-permute-done.4 = bf16[1,66,256]{2,1,0:T(8,128)(2,1)S(1)} collective-permute-done((bf16[1,66,256]{2,1,0:T(8,128)(2,1)S(1)}, bf16[1,66,256]{2,1,0:T(8,128)(2,1)S(1)}, u32[]{:S(2)}, u32[]{:S(2)}) %collective-permute-start.4) | collective-permute-done | bytes 33824 | tf_op jit(solution)/shard_map/ppermute | solution.py:34
  47.9 4.9 %collective-permute-done.5 = bf16[1,66,256]{2,1,0:T(8,128)(2,1)S(1)} collective-permute-done((bf16[1,66,256]{2,1,0:T(8,128)(2,1)S(1)}, bf16[1,66,256]{2,1,0:T(8,128)(2,1)S(1)}, u32[]{:S(2)}, u32[]{:S(2)}) %collective-permute-start.5) | collective-permute-done | bytes 33824 | tf_op jit(solution)/shard_map/ppermute | solution.py:34
  57.3 6.4 %collective-permute-start.7 = (bf16[1,66,256]{2,1,0:T(8,128)(2,1)S(1)}, bf16[1,66,256]{2,1,0:T(8,128)(2,1)S(1)}, u32[]{:S(2)}, u32[]{:S(2)}) collective-permute-start(bf16[1,66,256]{2,1,0:T(8,128)(2,1)S(1)} %fusion.14), channel_id=1, source_target_pairs={{0,128},{1,129},{2,130},{3,131},{4,132},{5,133},{6,134},{7,135},{1... | collective-permute-start | bytes 101384 | tf_op jit(solution)/shard_map/ppermute | solution.py:34
  82.1 6.8 %all-to-all-start = ((f32[16,1,544]{2,1,0:T(1,128)}), f32[16,1,544]{2,1,0:T(1,128)S(1)}, u32[]{:S(2)}, u32[]{:S(2)}) async-start(f32[16,1,544]{2,1,0:T(1,128)} %broadcast_in_dim.36), calls=%async_computation | async-start | bytes 81920 | tf_op jit(solution)/shard_map/all_to_all | solution.py:166
  90.2 5.1 %all-to-all-done = f32[16,1,544]{2,1,0:T(1,128)S(1)} async-done(((f32[16,1,544]{2,1,0:T(1,128)}), f32[16,1,544]{2,1,0:T(1,128)S(1)}, u32[]{:S(2)}, u32[]{:S(2)}) %all-to-all-start) | async-done | bytes 34848 | tf_op jit(solution)/shard_map/all_to_all | solution.py:166
  107.7 4.3 %pad_maximum_fusion = bf16[256,7168]{1,0:T(8,128)(2,1)} fusion(bf16[256,3584]{1,0:T(8,128)(2,1)} %param.21, bf16[256,3584]{1,0:T(8,128)(2,1)} %param.20), kind=kLoop, calls=%fused_computation.8 | loop fusion | flops 7340032 | bytes 7340032 | tf_op jit(solution)/shard_map/concatenate | solution.py:88
  112.8 13.0 %all-to-all-done.1 = f32[16,16,1280]{2,1,0:T(8,128)S(1)} async-done(((f32[16,16,1280]{2,1,0:T(8,128)}), f32[16,16,1280]{2,1,0:T(8,128)S(1)}, u32[]{:S(2)}, u32[]{:S(2)}) %all-to-all-start.1) | async-done | bytes 1310752 | tf_op jit(solution)/shard_map/all_to_all | solution.py:69
  130.7 4.5 %all-to-all-start.2 = ((bf16[16,16,1024]{2,1,0:T(8,128)(2,1)}), bf16[16,16,1024]{2,1,0:T(8,128)(2,1)S(1)}, u32[]{:S(2)}, u32[]{:S(2)}) async-start(bf16[16,16,1024]{2,1,0:T(8,128)(2,1)} %broadcast_in_dim.40), calls=%async_computation.2 | async-start | bytes 1048576 | tf_op jit(solution)/shard_map/all_to_all | solution.py:56
  135.2 9.3 %all-to-all-done.2 = bf16[16,16,1024]{2,1,0:T(8,128)(2,1)S(1)} async-done(((bf16[16,16,1024]{2,1,0:T(8,128)(2,1)}), bf16[16,16,1024]{2,1,0:T(8,128)(2,1)S(1)}, u32[]{:S(2)}, u32[]{:S(2)}) %all-to-all-start.2) | async-done | bytes 524320 | tf_op jit(solution)/shard_map/all_to_all | solution.py:56
  144.6 7.4 %all_to_all.55 = bf16[2,16,16,1024]{3,2,1,0:T(8,128)(2,1)S(1)} all-to-all(bf16[2,16,16,1024]{3,2,1,0:T(8,128)(2,1)S(1)} %broadcast_in_dim.41), channel_id=1, replica_groups=mesh['group'=2,'dp'=16,'tensor'=8] {'group'}, dimensions={0} | all-to-all | bytes 2097152 | tf_op jit(solution)/shard_map/all_to_all | solution.py:60
  154.1 24.6 %all_to_all.56 = f32[8,64,256]{2,1,0:T(8,128)S(1)} all-to-all(f32[8,64,256]{2,1,0:T(8,128)S(1)} %bitcast.147), channel_id=1, replica_groups=mesh['group'=2,'dp'=16,'tensor'=8] {'tensor'}, dimensions={0} | all-to-all | bytes 1048576 | tf_op jit(solution)/shard_map/all_to_all | solution.py:94
  179.6 5.3 %all-to-all-start.5 = ((f32[32,1,64]{2,1,0:T(1,128)}), f32[32,1,64]{2,1,0:T(1,128)S(1)}, u32[]{:S(2)}, u32[]{:S(2)}) async-start(f32[32,1,64]{2,1,0:T(1,128)} %broadcast_in_dim.42), calls=%async_computation.5 | async-start | bytes 32768 | tf_op jit(solution)/shard_map/all_to_all | solution.py:46
  184.9 6.7 %all-to-all-done.5 = f32[32,1,64]{2,1,0:T(1,128)S(1)} async-done(((f32[32,1,64]{2,1,0:T(1,128)}), f32[32,1,64]{2,1,0:T(1,128)S(1)}, u32[]{:S(2)}, u32[]{:S(2)}) %all-to-all-start.5) | async-done | bytes 8224 | tf_op jit(solution)/shard_map/all_to_all | solution.py:46
  193.0 3.9 %collective-permute-start.28 = (bf16[1,64,256]{2,1,0:T(8,128)(2,1)S(1)}, bf16[1,64,256]{2,1,0:T(8,128)(2,1)S(1)}, u32[]{:S(2)}, u32[]{:S(2)}) collective-permute-start(bf16[1,64,256]{2,1,0:T(8,128)(2,1)S(1)} %bitcast.164), channel_id=1, source_target_pairs={{0,134},{1,135},{2,132},{3,133},{4,130},{5,131},{6,128},{7,129},{1... | collective-permute-start | bytes 98312 | tf_op jit(solution)/shard_map/ppermute | solution.py:34
  212.5 4.0 %collective-permute-done.18 = bf16[1,64,256]{2,1,0:T(8,128)(2,1)S(1)} collective-permute-done((bf16[1,64,256]{2,1,0:T(8,128)(2,1)S(1)}, bf16[1,64,256]{2,1,0:T(8,128)(2,1)S(1)}, u32[]{:S(2)}, u32[]{:S(2)}) %collective-permute-start.18) | collective-permute-done | bytes 32800 | tf_op jit(solution)/shard_map/ppermute | solution.py:34
  216.5 5.7 %collective-permute-done.19 = bf16[1,64,256]{2,1,0:T(8,128)(2,1)S(1)} collective-permute-done((bf16[1,64,256]{2,1,0:T(8,128)(2,1)S(1)}, bf16[1,64,256]{2,1,0:T(8,128)(2,1)S(1)}, u32[]{:S(2)}, u32[]{:S(2)}) %collective-permute-start.19) | collective-permute-done | bytes 32800 | tf_op jit(solution)/shard_map/ppermute | solution.py:34
  231.1 7.3 %collective-permute-start.22 = (bf16[1,64,256]{2,1,0:T(8,128)(2,1)S(1)}, bf16[1,64,256]{2,1,0:T(8,128)(2,1)S(1)}, u32[]{:S(2)}, u32[]{:S(2)}) collective-permute-start(bf16[1,64,256]{2,1,0:T(8,128)(2,1)S(1)} %bitcast.173), channel_id=1, source_target_pairs={{0,128},{1,129},{2,130},{3,131},{4,132},{5,133},{6,134},{7,135},{1... | collective-permute-start | bytes 98312 | tf_op jit(solution)/shard_map/ppermute | solution.py:34
  244.3 4.2 %collective-permute-done.24 = bf16[1,64,256]{2,1,0:T(8,128)(2,1)S(1)} collective-permute-done((bf16[1,64,256]{2,1,0:T(8,128)(2,1)S(1)}, bf16[1,64,256]{2,1,0:T(8,128)(2,1)S(1)}, u32[]{:S(2)}, u32[]{:S(2)}) %collective-permute-start.24) | collective-permute-done | bytes 32800 | tf_op jit(solution)/shard_map/ppermute | solution.py:34
  255.1 5.2 %convolution_convert_fusion = bf16[256,7168]{1,0:T(8,128)(2,1)S(1)} fusion(bf16[512,7168]{1,0:T(8,128)(2,1)} %all-gather.5.cloned.1.call-done, bf16[512,512]{1,0:T(8,128)(2,1)S(1)} %bitcast.154, s32[]{:T(128)S(6)} %select_n.47), kind=kOutput, calls=%fused_computation.6 | convolution fusion | flops 1880883200 | bytes 11272196 | tf_op jit(solution)/shard_map/dot_general | solution.py:193
  260.2 47.3 %all_to_all.57 = bf16[16,16,7168]{2,1,0:T(8,128)(2,1)S(1)} all-to-all(bf16[16,16,7168]{2,1,0:T(8,128)(2,1)S(1)} %bitcast.142), channel_id=1, replica_groups=mesh['group'=2,'dp'=16,'tensor'=8] {'dp'}, dimensions={0} | all-to-all | bytes 7340032 | tf_op jit(solution)/shard_map/all_to_all | solution.py:69
  308.3 27.2 %all_to_all.58 = bf16[16,16,3584]{2,1,0:T(8,128)(2,1)S(1)} all-to-all(bf16[16,16,3584]{2,1,0:T(8,128)(2,1)S(1)} %broadcast_in_dim.43), channel_id=1, replica_groups=mesh['group'=2,'dp'=16,'tensor'=8] {'dp'}, dimensions={0} | all-to-all | bytes 3670016 | tf_op jit(solution)/shard_map/all_to_all | solution.py:56
  335.9 8.8 %all_to_all.59 = bf16[2,16,16,3584]{3,2,1,0:T(8,128)(2,1)S(1)} all-to-all(bf16[2,16,16,3584]{3,2,1,0:T(8,128)(2,1)S(1)} %broadcast_in_dim.44), channel_id=1, replica_groups=mesh['group'=2,'dp'=16,'tensor'=8] {'group'}, dimensions={0} | all-to-all | bytes 7340032 | tf_op jit(solution)/shard_map/all_to_all | solution.py:60
  345.8 19.4 %all_to_all.60 = f32[8,64,256]{2,1,0:T(8,128)S(1)} all-to-all(f32[8,64,256]{2,1,0:T(8,128)S(1)} %fusion), channel_id=1, replica_groups=mesh['group'=2,'dp'=16,'tensor'=8] {'tensor'}, dimensions={0} | all-to-all | bytes 1048576 | tf_op jit(solution)/shard_map/all_to_all | solution.py:94
  (170 shorter events, 115.0 us)
Async XLA Ops:
  6.5 94.5 %all-gather.3.cloned.1.call-start = ((), (), s32[]{:S(2)}) async-start(), calls=%async_computation.10 | async-start | bytes 1966080 | tf_op jit(solution)/shard_map/all_gather | solution.py:88
  8.8 68.8 %collective-permute-start.14 = (bf16[1,66,256]{2,1,0:T(8,128)(2,1)S(1)}, bf16[1,66,256]{2,1,0:T(8,128)(2,1)S(1)}, u32[]{:S(2)}, u32[]{:S(2)}) collective-permute-start(bf16[1,66,256]{2,1,0:T(8,128)(2,1)S(1)} %fusion.14), channel_id=1, source_target_pairs={{0,135},{1,134},{2,133},{3,132},{4,131},{5,130},{6,129},{7,128},{1... | collective-permute-start | bytes 101384 | tf_op jit(solution)/shard_map/ppermute | solution.py:34
  15.8 61.8 %collective-permute-start.13 = (bf16[1,66,256]{2,1,0:T(8,128)(2,1)S(1)}, bf16[1,66,256]{2,1,0:T(8,128)(2,1)S(1)}, u32[]{:S(2)}, u32[]{:S(2)}) collective-permute-start(bf16[1,66,256]{2,1,0:T(8,128)(2,1)S(1)} %fusion.14), channel_id=1, source_target_pairs={{0,134},{1,135},{2,132},{3,133},{4,130},{5,131},{6,128},{7,129},{1... | collective-permute-start | bytes 101384 | tf_op jit(solution)/shard_map/ppermute | solution.py:34
  16.3 61.3 %collective-permute-start.12 = (bf16[1,66,256]{2,1,0:T(8,128)(2,1)S(1)}, bf16[1,66,256]{2,1,0:T(8,128)(2,1)S(1)}, u32[]{:S(2)}, u32[]{:S(2)}) collective-permute-start(bf16[1,66,256]{2,1,0:T(8,128)(2,1)S(1)} %fusion.14), channel_id=1, source_target_pairs={{0,133},{1,132},{2,135},{3,134},{4,129},{5,128},{6,131},{7,130},{1... | collective-permute-start | bytes 101384 | tf_op jit(solution)/shard_map/ppermute | solution.py:34
  20.1 57.5 %collective-permute-start.11 = (bf16[1,66,256]{2,1,0:T(8,128)(2,1)S(1)}, bf16[1,66,256]{2,1,0:T(8,128)(2,1)S(1)}, u32[]{:S(2)}, u32[]{:S(2)}) collective-permute-start(bf16[1,66,256]{2,1,0:T(8,128)(2,1)S(1)} %fusion.14), channel_id=1, source_target_pairs={{0,132},{1,133},{2,134},{3,135},{4,128},{5,129},{6,130},{7,131},{1... | collective-permute-start | bytes 101384 | tf_op jit(solution)/shard_map/ppermute | solution.py:34
  35.0 7.0 %collective-permute-start.3 = (bf16[1,66,256]{2,1,0:T(8,128)(2,1)S(1)}, bf16[1,66,256]{2,1,0:T(8,128)(2,1)S(1)}, u32[]{:S(2)}, u32[]{:S(2)}) collective-permute-start(bf16[1,66,256]{2,1,0:T(8,128)(2,1)S(1)} %fusion.14), channel_id=1, source_target_pairs={{0,4},{1,5},{2,6},{3,7},{4,0},{5,1},{6,2},{7,3},{128,132},{129,133... | collective-permute-start | bytes 101384 | tf_op jit(solution)/shard_map/ppermute | solution.py:34
  42.1 5.9 %collective-permute-start.4 = (bf16[1,66,256]{2,1,0:T(8,128)(2,1)S(1)}, bf16[1,66,256]{2,1,0:T(8,128)(2,1)S(1)}, u32[]{:S(2)}, u32[]{:S(2)}) collective-permute-start(bf16[1,66,256]{2,1,0:T(8,128)(2,1)S(1)} %fusion.14), channel_id=1, source_target_pairs={{0,5},{1,4},{2,7},{3,6},{4,1},{5,0},{6,3},{7,2},{128,133},{129,132... | collective-permute-start | bytes 101384 | tf_op jit(solution)/shard_map/ppermute | solution.py:34
  57.3 7.3 %collective-permute-start.7 = (bf16[1,66,256]{2,1,0:T(8,128)(2,1)S(1)}, bf16[1,66,256]{2,1,0:T(8,128)(2,1)S(1)}, u32[]{:S(2)}, u32[]{:S(2)}) collective-permute-start(bf16[1,66,256]{2,1,0:T(8,128)(2,1)S(1)} %fusion.14), channel_id=1, source_target_pairs={{0,128},{1,129},{2,130},{3,131},{4,132},{5,133},{6,134},{7,135},{1... | collective-permute-start | bytes 101384 | tf_op jit(solution)/shard_map/ppermute | solution.py:34
  72.4 5.2 %collective-permute-start.10 = (bf16[1,66,256]{2,1,0:T(8,128)(2,1)S(1)}, bf16[1,66,256]{2,1,0:T(8,128)(2,1)S(1)}, u32[]{:S(2)}, u32[]{:S(2)}) collective-permute-start(bf16[1,66,256]{2,1,0:T(8,128)(2,1)S(1)} %fusion.14), channel_id=1, source_target_pairs={{0,131},{1,130},{2,129},{3,128},{4,135},{5,134},{6,133},{7,132},{1... | collective-permute-start | bytes 101384 | tf_op jit(solution)/shard_map/ppermute | solution.py:34
  82.1 13.2 %all-to-all-start = ((f32[16,1,544]{2,1,0:T(1,128)}), f32[16,1,544]{2,1,0:T(1,128)S(1)}, u32[]{:S(2)}, u32[]{:S(2)}) async-start(f32[16,1,544]{2,1,0:T(1,128)} %broadcast_in_dim.36), calls=%async_computation | async-start | bytes 81920 | tf_op jit(solution)/shard_map/all_to_all | solution.py:166
  104.0 21.8 %all-to-all-start.1 = ((f32[16,16,1280]{2,1,0:T(8,128)}), f32[16,16,1280]{2,1,0:T(8,128)S(1)}, u32[]{:S(2)}, u32[]{:S(2)}) async-start(f32[16,16,1280]{2,1,0:T(8,128)} %bitcast.26), calls=%async_computation.1 | async-start | bytes 2621440 | tf_op jit(solution)/shard_map/all_to_all | solution.py:69
  107.7 147.4 %all-gather.5.cloned.1.call-start = ((), (), s32[]{:S(2)}) async-start(), calls=%async_computation.11 | async-start | bytes 11010048 | tf_op jit(solution)/shard_map/all_gather | solution.py:88
  130.7 13.8 %all-to-all-start.2 = ((bf16[16,16,1024]{2,1,0:T(8,128)(2,1)}), bf16[16,16,1024]{2,1,0:T(8,128)(2,1)S(1)}, u32[]{:S(2)}, u32[]{:S(2)}) async-start(bf16[16,16,1024]{2,1,0:T(8,128)(2,1)} %broadcast_in_dim.40), calls=%async_computation.2 | async-start | bytes 1048576 | tf_op jit(solution)/shard_map/all_to_all | solution.py:56
  179.6 12.1 %all-to-all-start.5 = ((f32[32,1,64]{2,1,0:T(1,128)}), f32[32,1,64]{2,1,0:T(1,128)S(1)}, u32[]{:S(2)}, u32[]{:S(2)}) async-start(f32[32,1,64]{2,1,0:T(1,128)} %broadcast_in_dim.42), calls=%async_computation.5 | async-start | bytes 32768 | tf_op jit(solution)/shard_map/all_to_all | solution.py:46
  191.8 9.0 %collective-permute-start.15 = (bf16[1,64,256]{2,1,0:T(8,128)(2,1)S(1)}, bf16[1,64,256]{2,1,0:T(8,128)(2,1)S(1)}, u32[]{:S(2)}, u32[]{:S(2)}) collective-permute-start(bf16[1,64,256]{2,1,0:T(8,128)(2,1)S(1)} %bitcast.162), channel_id=1, source_target_pairs={{0,1},{1,0},{2,3},{3,2},{4,5},{5,4},{6,7},{7,6},{128,129},{129,128... | collective-permute-start | bytes 98312 | tf_op jit(solution)/shard_map/ppermute | solution.py:34
  192.2 61.6 %collective-permute-start.29 = (bf16[1,64,256]{2,1,0:T(8,128)(2,1)S(1)}, bf16[1,64,256]{2,1,0:T(8,128)(2,1)S(1)}, u32[]{:S(2)}, u32[]{:S(2)}) collective-permute-start(bf16[1,64,256]{2,1,0:T(8,128)(2,1)S(1)} %bitcast.163), channel_id=1, source_target_pairs={{0,135},{1,134},{2,133},{3,132},{4,131},{5,130},{6,129},{7,128},{1... | collective-permute-start | bytes 98312 | tf_op jit(solution)/shard_map/ppermute | solution.py:34
  193.0 60.7 %collective-permute-start.28 = (bf16[1,64,256]{2,1,0:T(8,128)(2,1)S(1)}, bf16[1,64,256]{2,1,0:T(8,128)(2,1)S(1)}, u32[]{:S(2)}, u32[]{:S(2)}) collective-permute-start(bf16[1,64,256]{2,1,0:T(8,128)(2,1)S(1)} %bitcast.164), channel_id=1, source_target_pairs={{0,134},{1,135},{2,132},{3,133},{4,130},{5,131},{6,128},{7,129},{1... | collective-permute-start | bytes 98312 | tf_op jit(solution)/shard_map/ppermute | solution.py:34
  196.9 56.8 %collective-permute-start.27 = (bf16[1,64,256]{2,1,0:T(8,128)(2,1)S(1)}, bf16[1,64,256]{2,1,0:T(8,128)(2,1)S(1)}, u32[]{:S(2)}, u32[]{:S(2)}) collective-permute-start(bf16[1,64,256]{2,1,0:T(8,128)(2,1)S(1)} %bitcast.165), channel_id=1, source_target_pairs={{0,133},{1,132},{2,135},{3,134},{4,129},{5,128},{6,131},{7,130},{1... | collective-permute-start | bytes 98312 | tf_op jit(solution)/shard_map/ppermute | solution.py:34
  197.2 56.5 %collective-permute-start.26 = (bf16[1,64,256]{2,1,0:T(8,128)(2,1)S(1)}, bf16[1,64,256]{2,1,0:T(8,128)(2,1)S(1)}, u32[]{:S(2)}, u32[]{:S(2)}) collective-permute-start(bf16[1,64,256]{2,1,0:T(8,128)(2,1)S(1)} %bitcast.166), channel_id=1, source_target_pairs={{0,132},{1,133},{2,134},{3,135},{4,128},{5,129},{6,130},{7,131},{1... | collective-permute-start | bytes 98312 | tf_op jit(solution)/shard_map/ppermute | solution.py:34
  209.8 6.7 %collective-permute-start.18 = (bf16[1,64,256]{2,1,0:T(8,128)(2,1)S(1)}, bf16[1,64,256]{2,1,0:T(8,128)(2,1)S(1)}, u32[]{:S(2)}, u32[]{:S(2)}) collective-permute-start(bf16[1,64,256]{2,1,0:T(8,128)(2,1)S(1)} %bitcast.169), channel_id=1, source_target_pairs={{0,4},{1,5},{2,6},{3,7},{4,0},{5,1},{6,2},{7,3},{128,132},{129,133... | collective-permute-start | bytes 98312 | tf_op jit(solution)/shard_map/ppermute | solution.py:34
  216.5 5.8 %collective-permute-start.19 = (bf16[1,64,256]{2,1,0:T(8,128)(2,1)S(1)}, bf16[1,64,256]{2,1,0:T(8,128)(2,1)S(1)}, u32[]{:S(2)}, u32[]{:S(2)}) collective-permute-start(bf16[1,64,256]{2,1,0:T(8,128)(2,1)S(1)} %bitcast.170), channel_id=1, source_target_pairs={{0,5},{1,4},{2,7},{3,6},{4,1},{5,0},{6,3},{7,2},{128,133},{129,132... | collective-permute-start | bytes 98312 | tf_op jit(solution)/shard_map/ppermute | solution.py:34
  231.1 8.2 %collective-permute-start.22 = (bf16[1,64,256]{2,1,0:T(8,128)(2,1)S(1)}, bf16[1,64,256]{2,1,0:T(8,128)(2,1)S(1)}, u32[]{:S(2)}, u32[]{:S(2)}) collective-permute-start(bf16[1,64,256]{2,1,0:T(8,128)(2,1)S(1)} %bitcast.173), channel_id=1, source_target_pairs={{0,128},{1,129},{2,130},{3,131},{4,132},{5,133},{6,134},{7,135},{1... | collective-permute-start | bytes 98312 | tf_op jit(solution)/shard_map/ppermute | solution.py:34
  239.3 5.1 %collective-permute-start.23 = (bf16[1,64,256]{2,1,0:T(8,128)(2,1)S(1)}, bf16[1,64,256]{2,1,0:T(8,128)(2,1)S(1)}, u32[]{:S(2)}, u32[]{:S(2)}) collective-permute-start(bf16[1,64,256]{2,1,0:T(8,128)(2,1)S(1)} %bitcast.174), channel_id=1, source_target_pairs={{0,129},{1,128},{2,131},{3,130},{4,133},{5,132},{6,135},{7,134},{1... | collective-permute-start | bytes 98312 | tf_op jit(solution)/shard_map/ppermute | solution.py:34
  248.6 5.1 %collective-permute-start.25 = (bf16[1,64,256]{2,1,0:T(8,128)(2,1)S(1)}, bf16[1,64,256]{2,1,0:T(8,128)(2,1)S(1)}, u32[]{:S(2)}, u32[]{:S(2)}) collective-permute-start(bf16[1,64,256]{2,1,0:T(8,128)(2,1)S(1)} %bitcast.176), channel_id=1, source_target_pairs={{0,131},{1,130},{2,129},{3,128},{4,135},{5,134},{6,133},{7,132},{1... | collective-permute-start | bytes 98312 | tf_op jit(solution)/shard_map/ppermute | solution.py:34
  (17 other events, 466.8 us)
Sparse Core Ops, SparseCore 0:
  24.4 16.3 all-gather.2
  112.2 25.7 all-gather.4
